TPU v7x, 32 devices: a whole 2x2x4 slice. The times are simulated.
32 devices in a mesh: grp: 2 (over y), gx: 16 (over z, x, core).
Axes of the slice: x: 2, y: 2, z: 4, core: 2. Of those that a mesh axis runs over, the one named last changes fastest.
Arguments:
- volume: float32 [512, 896], P(('grp', 'gx')), parts along dimension 0, may hold values from -45 to 45
- bank: float32 [8, 4096], P(None, 'gx'), may hold values from -43 to 43
- orient: int32 [8], replicated, may hold values from 0 to 47
- bank_id: int32 [8], replicated, may hold values from 0 to 7, each once
- counts: int32 [8], replicated, may hold values from 1 to 16
Outputs:
- fields: float32 [4, 512, 896], P(None, ('grp', 'gx')), parts along dimension 1
There are 2 independent parts, one for each index of `grp`. A program takes and returns all parts, laid end to end along the dimension named above; an argument that names none is the same for every part. Nothing has to cross between parts.
Inputs may be any that keep to these rules, and one draw needn't show every extreme that they name: `bank_id`: each of the 8 base templates is named by exactly one list entry.
All inputs are finite; a program needn't handle non-finite values.
Results may differ from a plain program's by a relative error of at most 0.0003.
Values sent between devices are 32-bit elements; how exact they have to be, the bound alone decides.
No kernel may reach another device: no remote copies, remote signals or barrier semaphores. Data moves between devices by JAX's collectives and lax.ppermute only.
A program may use at most 64 MiB of HBM per device.

v0:
```python
import math
import jax
import jax.numpy as jnp
import numpy as np
from jax import lax
from jax.sharding import PartitionSpec as P

BY = 8
BZ = 112
TS = 16
NT = 8
FIELDS = 4
epsilon = 1e-05
sharpness = 80.0
AXIS_ORDERS = np.array([[0, 1, 2], [0, 2, 1], [1, 0, 2], [1, 2, 0], [2, 0, 1], [2, 1, 0]], np.int32)


def extended(x, sides, width):
    for axis, dim in sides:
        size, length = (lax.axis_size(axis), x.shape[dim])
        up = [(i, (i + 1) % size) for i in range(size - 1)]
        down = [(j, i) for i, j in up]
        last = lax.slice_in_dim(x, length - width, length, axis=dim)
        leading = lax.slice_in_dim(x, 0, width, axis=dim)
        before = lax.ppermute(last, axis, up)
        after = lax.ppermute(leading, axis, down)
        x = jnp.concatenate([before, x, after], axis=dim)
    return x


def padded_length(length):
    return -(-length // 128) * 128


def rotate_template(flat_base, orient_one):
    coords = jnp.arange(TS**3, dtype=jnp.int32)
    index_set = jnp.stack([coords // (TS * TS), coords // TS % TS, coords % TS])
    order_row = orient_one // 8
    flip_set = orient_one % 8
    picked = (jnp.arange(6, dtype=jnp.int32) == order_row).astype(jnp.int32)
    ordering = jnp.sum(picked[:, None] * jnp.asarray(AXIS_ORDERS), axis=0)
    source = jnp.zeros_like(coords)
    for axis_num in range(3):
        select = (ordering[axis_num] == jnp.arange(3, dtype=jnp.int32)).astype(jnp.int32)
        chosen = jnp.sum(select[:, None] * index_set, axis=0)
        flipped = flip_set // 2**axis_num % 2
        placed = chosen + flipped * (TS - 1 - 2 * chosen)
        source = source * TS + placed
    return flat_base[source]


def normalized_kernel(flat_base, orient_one):
    rotated = rotate_template(flat_base, orient_one)
    centered = rotated - jnp.mean(rotated)
    return centered / jnp.sqrt(jnp.sum(centered * centered) + epsilon)


def wave_tables(positions, targets, period, direction):
    turns = (positions[:, None] * targets[None, :] % period).astype(jnp.float32)
    phase = 2.0 * math.pi / period * turns
    return (jnp.cos(phase), direction * jnp.sin(phase))


def band_table(positions, targets, period):
    offset = (positions[:, None] - targets[None, :]) % period
    return (offset < TS).astype(jnp.float32)


def contract(letters, data, table):
    return jnp.einsum(letters, data, table, precision=lax.Precision.HIGHEST)


def spectrum_along(real_part, imag_part, cos_table, sin_table, letters):
    new_real = contract(letters, real_part, cos_table) - contract(letters, imag_part, sin_table)
    new_imag = contract(letters, real_part, sin_table) + contract(letters, imag_part, cos_table)
    return (new_real, new_imag)


def local(volume, bank, orient, bank_id, counts):
    rows_x = volume.shape[0]
    half = TS // 2
    grid = volume.reshape(rows_x, BY, BZ)
    len_x = rows_x + TS
    len_y = BY + TS
    len_z = padded_length(BZ + TS)
    gathered = lax.all_gather(bank, "gx", axis=1, tiled=True)
    kernels = jax.vmap(normalized_kernel)(gathered[bank_id], orient)
    field_in = extended(grid, (("gx", 0),), half)
    pos_x = jnp.arange(len_x, dtype=jnp.int32)
    out_x = jnp.arange(rows_x, dtype=jnp.int32)
    pos_y = half + jnp.arange(BY, dtype=jnp.int32)
    pos_z = half + jnp.arange(BZ, dtype=jnp.int32)
    freq_x = jnp.arange(len_x, dtype=jnp.int32)
    freq_y = jnp.arange(len_y, dtype=jnp.int32)
    freq_z = jnp.arange(len_z, dtype=jnp.int32)
    tmpl_pos = jnp.arange(TS, dtype=jnp.int32)
    cos_z, sin_z = wave_tables(pos_z, freq_z, len_z, -1.0)
    cos_y, sin_y = wave_tables(pos_y, freq_y, len_y, -1.0)
    cos_x, sin_x = wave_tables(pos_x, freq_x, len_x, -1.0)
    vol_re = contract("xyz,zk->xyk", field_in, cos_z)
    vol_im = contract("xyz,zk->xyk", field_in, sin_z)
    vol_re, vol_im = spectrum_along(vol_re, vol_im, cos_y, sin_y, "xyk,yj->xjk")
    vol_re, vol_im = spectrum_along(vol_re, vol_im, cos_x, sin_x, "xjk,xi->ijk")
    kcos_z, ksin_z = wave_tables(tmpl_pos, freq_z, len_z, -1.0)
    kcos_y, ksin_y = wave_tables(tmpl_pos, freq_y, len_y, -1.0)
    kcos_x, ksin_x = wave_tables(tmpl_pos, freq_x, len_x, -1.0)
    icos_y, isin_y = wave_tables(freq_y, jnp.arange(BY, dtype=jnp.int32), len_y, 1.0)
    icos_x, isin_x = wave_tables(freq_x, out_x, len_x, 1.0)
    icos_z, isin_z = wave_tables(freq_z, jnp.arange(BZ, dtype=jnp.int32), len_z, 1.0)
    inverse_scale = 1.0 / (len_x * len_y * len_z)

    def correlate(kernel_flat):
        kernel = kernel_flat.reshape(TS, TS, TS)
        kernel_re = contract("xyz,zk->xyk", kernel, kcos_z)
        kernel_im = contract("xyz,zk->xyk", kernel, ksin_z)
        kernel_re, kernel_im = spectrum_along(kernel_re, kernel_im, kcos_y, ksin_y, "xyk,yj->xjk")
        kernel_re, kernel_im = spectrum_along(kernel_re, kernel_im, kcos_x, ksin_x, "xjk,xi->ijk")
        prod_re = kernel_re * vol_re + kernel_im * vol_im
        prod_im = kernel_re * vol_im - kernel_im * vol_re
        prod_re, prod_im = spectrum_along(prod_re, prod_im, icos_y, isin_y, "ijk,jn->ink")
        prod_re, prod_im = spectrum_along(prod_re, prod_im, icos_x, isin_x, "ink,im->mnk")
        real_out = contract("mnk,kz->mnz", prod_re, icos_z) - contract(
            "mnk,kz->mnz", prod_im, isin_z
        )
        return real_out * inverse_scale

    numer = lax.map(correlate, kernels)
    squares = field_in * field_in
    energy = contract(
        "xyz,zn->xyn", squares, band_table(pos_z, jnp.arange(BZ, dtype=jnp.int32), len_z)
    )
    energy = contract(
        "xyn,ym->xmn", energy, band_table(pos_y, jnp.arange(BY, dtype=jnp.int32), len_y)
    )
    energy = contract("xmn,xl->lmn", energy, band_table(pos_x, out_x, len_x))
    scores = numer / jnp.sqrt(energy + epsilon)[None]
    weights = counts.astype(jnp.float32)
    weighted = weights[:, None, None, None] * jnp.exp(sharpness * scores)
    grouped = jnp.sum(weighted.reshape(FIELDS, NT // FIELDS, rows_x, BY, BZ), axis=1)
    totals = jnp.sum(weights.reshape(FIELDS, NT // FIELDS), axis=1)
    fields = jnp.log(grouped / totals[:, None, None, None])
    return fields.reshape(FIELDS, rows_x, BY * BZ)


def solution(mesh):
    in_specs = (P(("grp", "gx"), None), P(None, "gx"), P(), P(), P())
    out_specs = P(None, ("grp", "gx"), None)
    return jax.shard_map(local, mesh=mesh, in_specs=in_specs, out_specs=out_specs, check_vma=False)
```

profile of v0, /device:TPU:0, one launch (start us, length us, event | category | flops | bytes accessed | tf_op | source)
XLA Modules:
  0.0 316.0 jit_solution(17705312637097414959)
XLA Ops:
  0.0 0.8 fusion.433
  0.8 2.3 collective-permute-start
  3.3 1.3 collective-permute-start.1
  4.6 0.7 compare_select_fusion.3
  5.3 0.7 and_select_fusion.8
  6.1 0.8 multiply_reduce_fusion.4
  6.9 25.6 %all_gather.3 = f32[8,4096]{1,0:T(8,128)S(1)} all-gather(f32[8,256]{1,0:T(8,128)} %param.9), channel_id=1, replica_groups=mesh['grp'=2,'gx'=16] {'gx'}, dimensions={1}, use_global_device_ids=true | all-gather | bytes 139264 | tf_op jit(solution)/shard_map/all_gather | solution.py:86
  32.9 0.6 gather_fusion
  33.5 200.1 %gather_fusion.1 = f32[32768]{0:T(1024)S(1)} fusion(f32[8,4096]{1,0:T(8,128)S(1)} %gather_fusion, s32[32768]{0:T(1024)S(1)} %bitcast.250), kind=kCustom, calls=%fused_computation.1 | custom fusion | bytes 524288 | tf_op jit(solution)/shard_map/vmap()/gather | solution.py:49
  235.9 0.6 fusion.332
  236.6 0.6 fusion.336
  237.2 0.6 fusion.250
  239.8 0.6 fusion.249
  240.5 0.6 convolution_subtract_fusion.5
  241.6 73.3 %while.12 = (s32[]{:T(128)}, f32[8,16,8,112]{3,2,1,0:T(8,128)S(1)}, f32[8,4096]{1,0:T(8,128)S(1)}, f32[32,24,128]{2,0,1:T(8,128)S(1)}, f32[32,24,128]{2,0,1:T(8,128)S(1)}, /*index=5*/s32[]{:T(128)}) while((s32[]{:T(128)}, f32[8,16,8,112]{3,2,1,0:T(8,128)S(1)}, f32[8,4096]{1,0:T(8,128)S(1)}, ...), condition=%wide.region_7.8_spmd.clone.clone, body=%wide.region_6.7_spmd.clone.clone.sunk | while | flops 234336256 | bytes 10379349 | solution.py:127
  246.0 0.7 multiply_subtract_fusion.2
  255.1 0.7 multiply_subtract_fusion.2
  264.3 0.7 multiply_subtract_fusion.2
  273.4 0.7 multiply_subtract_fusion.2
  282.5 0.7 multiply_subtract_fusion.2
  291.7 0.7 multiply_subtract_fusion.2
  300.8 0.7 multiply_subtract_fusion.2
  310.0 0.7 multiply_subtract_fusion.2
  315.2 0.8 divide_log_fusion
  (216 shorter events, 71.7 us)
Async XLA Ops:
  0.8 233.9 %collective-permute-start = (f32[8,8,112]{2,1,0:T(8,128)S(1)}, f32[8,8,112]{2,1,0:T(8,128)S(1)}, u32[]{:S(2)}, u32[]{:S(2)}) collective-permute-start(f32[8,8,112]{2,1,0:T(8,128)S(1)} %slice.34), channel_id=1, source_target_pairs={{0,1},{1,2},{2,3},{3,4},{4,5},{5,6},{6,7},{7,8},{8,9},{9,10},{10,1... | collective-permute-start | bytes 86024 | tf_op jit(solution)/shard_map/ppermute | solution.py:25
  3.3 231.5 %collective-permute-start.1 = (f32[8,8,112]{2,1,0:T(8,128)S(1)}, f32[8,8,112]{2,1,0:T(8,128)S(1)}, u32[]{:S(2)}, u32[]{:S(2)}) collective-permute-start(f32[8,8,112]{2,1,0:T(8,128)S(1)} %slice.36), channel_id=1, source_target_pairs={{1,0},{2,1},{3,2},{4,3},{5,4},{6,5},{7,6},{8,7},{9,8},{10,9},{11,1... | collective-permute-start | bytes 86024 | tf_op jit(solution)/shard_map/ppermute | solution.py:26
  233.6 0.8 copy-start
  233.6 0.9 copy-start.1
where the time goes:
time: 316 us
  local copies, waits for them, and re-layouts  203 us (64%)
  matrix products  77.2 us (24%)
  blocking collectives  25.6 us (8%)
  other arithmetic  4.22 us (1%)
  starting transfers between devices  3.63 us (1%)
    gather x2, local copies, waits for them, and re-layouts, rotate_template(): return flat_base[source]  200 us
    dot_general x173, matrix products, contract(): return jnp.einsum(letters, data, table, precision=lax.Precision.HIGHEST)  77.2 us
    all_gather x1, blocking collectives, local(): gathered = lax.all_gather(bank, 'gx', axis=1, tiled=True)  25.6 us
  transfers between devices with their start and end apart: 2, of which 0 were waited for; matrix products, arithmetic and copies ran while one was open for 65% of the time, Pallas kernels for 0%

commit v1 on v0

--- a/solution.py
+++ b/solution.py
@@ -83,7 +83,16 @@
     len_x = rows_x + TS
     len_y = BY + TS
     len_z = padded_length(BZ + TS)
-    gathered = lax.all_gather(bank, "gx", axis=1, tiled=True)
+    local_now = lax.axis_size("gx")
+    arr_out, local_out, outcome_arr = (local_now, lax.axis_index("gx"), bank.shape[1])
+    xs_all = tuple(((m, (m + 1) % arr_out) for m in range(arr_out)))
+    gathered = jnp.zeros((*bank.shape[:1], arr_out * outcome_arr, *bank.shape[1 + 1 :]), bank.dtype)
+    v1 = bank
+    for dev_j in range(arr_out):
+        y2 = (local_out - dev_j) % arr_out
+        gathered = lax.dynamic_update_slice_in_dim(gathered, v1, y2 * outcome_arr, axis=1)
+        if dev_j < arr_out - 1:
+            v1 = lax.ppermute(v1, "gx", xs_all)
     kernels = jax.vmap(normalized_kernel)(gathered[bank_id], orient)
     field_in = extended(grid, (("gx", 0),), half)
     pos_x = jnp.arange(len_x, dtype=jnp.int32)

time: 316 us -> 368 us (1.16)
  waiting for transfers between devices: 0.01 us -> 73.9 us
  blocking collectives: 25.6 us -> 0 us
  starting transfers between devices: 3.63 us -> 7.5 us
    ppermute x0 -> x15, waiting for transfers between devices: none -> 73.9 us  [local(): v1 = lax.ppermute(v1, 'gx', xs_all)]
    all_gather x1 -> x0, blocking collectives: 25.6 us -> none  [local(): gathered = lax.all_gather(bank, 'gx', axis=1, tiled=True)]
  transfers between devices with their start and end apart: 2 -> 17, of which waited for: 0 -> 13; matrix products, arithmetic and copies ran while one was open for 65% -> 3% of each run, Pallas kernels for 0% -> 0%
where the time goes in v1:
time: 368 us
  local copies, waits for them, and re-layouts  203 us (55%)
  matrix products  77.2 us (21%)
  waiting for transfers between devices  73.9 us (20%)
  starting transfers between devices  7.5 us (2%)
    gather x2, local copies, waits for them, and re-layouts, rotate_template(): return flat_base[source]  200 us
    dot_general x173, matrix products, contract(): return jnp.einsum(letters, data, table, precision=lax.Precision.HIGHEST)  77.2 us
    ppermute x15, waiting for transfers between devices, local(): v1 = lax.ppermute(v1, 'gx', xs_all)  73.9 us
  transfers between devices with their start and end apart: 17, of which 13 were waited for; matrix products, arithmetic and copies ran while one was open for 3% of the time, Pallas kernels for 0%

profile of v1, /device:TPU:0, one launch (start us, length us, event | category | flops | bytes accessed | tf_op | source)
XLA Modules:
  0.0 367.8 jit_solution(6596251827792492727)
XLA Ops:
  0.5 0.8 fusion.428
  1.3 4.5 %collective-permute-start.15 = (f32[8,8,112]{2,1,0:T(8,128)S(1)}, f32[8,8,112]{2,1,0:T(8,128)S(1)}, u32[]{:S(2)}, u32[]{:S(2)}) collective-permute-start(f32[8,8,112]{2,1,0:T(8,128)S(1)} %slice.34), channel_id=1, source_target_pairs={{0,1},{1,2},{2,3},{3,4},{4,5},{5,6},{6,7},{7,8},{8,9},{9,10},{10,1... | collective-permute-start | bytes 86024 | tf_op jit(solution)/shard_map/ppermute | solution.py:25
  5.9 1.3 collective-permute-start.16
  10.4 1.2 collective-permute-start.1
  11.6 4.6 %collective-permute-done.1 = f32[8,256]{1,0:T(8,128)S(1)} collective-permute-done((f32[8,256]{1,0:T(8,128)S(1)}, f32[8,256]{1,0:T(8,128)S(1)}, u32[]{:S(2)}, u32[]{:S(2)}) %collective-permute-start.1) | collective-permute-done | bytes 8224 | tf_op jit(solution)/shard_map/ppermute | solution.py:95
  16.2 5.8 %collective-permute-done.2 = f32[8,256]{1,0:T(8,128)S(1)} collective-permute-done((f32[8,256]{1,0:T(8,128)S(1)}, f32[8,256]{1,0:T(8,128)S(1)}, u32[]{:S(2)}, u32[]{:S(2)}) %collective-permute-start.2) | collective-permute-done | bytes 8224 | tf_op jit(solution)/shard_map/ppermute | solution.py:95
  28.9 5.8 %collective-permute-done.4 = f32[8,256]{1,0:T(8,128)S(1)} collective-permute-done((f32[8,256]{1,0:T(8,128)S(1)}, f32[8,256]{1,0:T(8,128)S(1)}, u32[]{:S(2)}, u32[]{:S(2)}) %collective-permute-start.4) | collective-permute-done | bytes 8224 | tf_op jit(solution)/shard_map/ppermute | solution.py:95
  34.7 5.8 %collective-permute-done.5 = f32[8,256]{1,0:T(8,128)S(1)} collective-permute-done((f32[8,256]{1,0:T(8,128)S(1)}, f32[8,256]{1,0:T(8,128)S(1)}, u32[]{:S(2)}, u32[]{:S(2)}) %collective-permute-start.5) | collective-permute-done | bytes 8224 | tf_op jit(solution)/shard_map/ppermute | solution.py:95
  40.5 5.8 %collective-permute-done.6 = f32[8,256]{1,0:T(8,128)S(1)} collective-permute-done((f32[8,256]{1,0:T(8,128)S(1)}, f32[8,256]{1,0:T(8,128)S(1)}, u32[]{:S(2)}, u32[]{:S(2)}) %collective-permute-start.6) | collective-permute-done | bytes 8224 | tf_op jit(solution)/shard_map/ppermute | solution.py:95
  46.3 5.8 %collective-permute-done.7 = f32[8,256]{1,0:T(8,128)S(1)} collective-permute-done((f32[8,256]{1,0:T(8,128)S(1)}, f32[8,256]{1,0:T(8,128)S(1)}, u32[]{:S(2)}, u32[]{:S(2)}) %collective-permute-start.7) | collective-permute-done | bytes 8224 | tf_op jit(solution)/shard_map/ppermute | solution.py:95
  52.0 5.8 %collective-permute-done.8 = f32[8,256]{1,0:T(8,128)S(1)} collective-permute-done((f32[8,256]{1,0:T(8,128)S(1)}, f32[8,256]{1,0:T(8,128)S(1)}, u32[]{:S(2)}, u32[]{:S(2)}) %collective-permute-start.8) | collective-permute-done | bytes 8224 | tf_op jit(solution)/shard_map/ppermute | solution.py:95
  57.8 5.8 %collective-permute-done.9 = f32[8,256]{1,0:T(8,128)S(1)} collective-permute-done((f32[8,256]{1,0:T(8,128)S(1)}, f32[8,256]{1,0:T(8,128)S(1)}, u32[]{:S(2)}, u32[]{:S(2)}) %collective-permute-start.9) | collective-permute-done | bytes 8224 | tf_op jit(solution)/shard_map/ppermute | solution.py:95
  63.6 5.8 %collective-permute-done.10 = f32[8,256]{1,0:T(8,128)S(1)} collective-permute-done((f32[8,256]{1,0:T(8,128)S(1)}, f32[8,256]{1,0:T(8,128)S(1)}, u32[]{:S(2)}, u32[]{:S(2)}) %collective-permute-start.10) | collective-permute-done | bytes 8224 | tf_op jit(solution)/shard_map/ppermute | solution.py:95
  69.4 5.8 %collective-permute-done.11 = f32[8,256]{1,0:T(8,128)S(1)} collective-permute-done((f32[8,256]{1,0:T(8,128)S(1)}, f32[8,256]{1,0:T(8,128)S(1)}, u32[]{:S(2)}, u32[]{:S(2)}) %collective-permute-start.11) | collective-permute-done | bytes 8224 | tf_op jit(solution)/shard_map/ppermute | solution.py:95
  75.1 5.8 %collective-permute-done.12 = f32[8,256]{1,0:T(8,128)S(1)} collective-permute-done((f32[8,256]{1,0:T(8,128)S(1)}, f32[8,256]{1,0:T(8,128)S(1)}, u32[]{:S(2)}, u32[]{:S(2)}) %collective-permute-start.12) | collective-permute-done | bytes 8224 | tf_op jit(solution)/shard_map/ppermute | solution.py:95
  80.9 5.8 %collective-permute-done.13 = f32[8,256]{1,0:T(8,128)S(1)} collective-permute-done((f32[8,256]{1,0:T(8,128)S(1)}, f32[8,256]{1,0:T(8,128)S(1)}, u32[]{:S(2)}, u32[]{:S(2)}) %collective-permute-start.13) | collective-permute-done | bytes 8224 | tf_op jit(solution)/shard_map/ppermute | solution.py:95
  86.7 5.8 %collective-permute-done.14 = f32[8,256]{1,0:T(8,128)S(1)} collective-permute-done((f32[8,256]{1,0:T(8,128)S(1)}, f32[8,256]{1,0:T(8,128)S(1)}, u32[]{:S(2)}, u32[]{:S(2)}) %collective-permute-start.14) | collective-permute-done | bytes 8224 | tf_op jit(solution)/shard_map/ppermute | solution.py:95
  93.0 200.1 %gather_fusion.1 = f32[32768]{0:T(1024)S(1)} fusion(f32[8,4096]{1,0:T(8,128)S(1)} %gather_fusion, s32[32768]{0:T(1024)S(1)} %bitcast.250), kind=kCustom, calls=%fused_computation.1 | custom fusion | bytes 524288 | tf_op jit(solution)/shard_map/vmap()/gather | solution.py:49
  293.7 73.1 %while.12 = (s32[]{:T(128)}, f32[8,16,8,112]{3,2,1,0:T(8,128)S(1)}, f32[8,4096]{1,0:T(8,128)S(1)}, f32[32,24,128]{2,0,1:T(8,128)S(1)}, f32[32,24,128]{2,0,1:T(8,128)S(1)}, /*index=5*/s32[]{:T(128)}) while((s32[]{:T(128)}, f32[8,16,8,112]{3,2,1,0:T(8,128)S(1)}, f32[8,4096]{1,0:T(8,128)S(1)}, ...), condition=%wide.region_7.8_spmd.clone.clone, body=%wide.region_6.7_spmd.clone.clone.sunk | while | flops 234336256 | bytes 10379349 | solution.py:136
  297.9 0.7 multiply_subtract_fusion.2
  316.1 0.7 multiply_subtract_fusion.2
  325.3 0.7 multiply_subtract_fusion.2
  334.4 0.7 multiply_subtract_fusion.2
  367.0 0.8 divide_log_fusion
  (266 shorter events, 80.3 us)
Async XLA Ops:
  0.0 8.8 %copy-start.2 = (s32[6,3]{0,1:T(4,128)S(1)}, s32[6,3]{0,1:T(4,128)}, u32[]{:S(2)}) copy-start(s32[6,3]{0,1:T(4,128)} %constant.390.clone) | copy-start | bytes 220
  0.0 9.0 %copy-start.1 = (f32[8,256]{1,0:T(8,128)S(1)}, f32[8,256]{1,0:T(8,128)}, u32[]{:S(2)}) copy-start(f32[8,256]{1,0:T(8,128)} %param.9) | copy-start | bytes 24580
  0.0 10.4 %collective-permute-start = (f32[8,256]{1,0:T(8,128)}, f32[8,256]{1,0:T(8,128)S(1)}, u32[]{:S(2)}, u32[]{:S(2)}) collective-permute-start(f32[8,256]{1,0:T(8,128)} %param.9), channel_id=1, source_target_pairs={{0,1},{1,2},{2,3},{3,4},{4,5},{5,6},{6,7},{7,8},{8,9},{9,10},{10,1... | collective-permute-start | bytes 24584 | tf_op jit(solution)/shard_map/ppermute | solution.py:95
  1.3 20.7 %collective-permute-start.15 = (f32[8,8,112]{2,1,0:T(8,128)S(1)}, f32[8,8,112]{2,1,0:T(8,128)S(1)}, u32[]{:S(2)}, u32[]{:S(2)}) collective-permute-start(f32[8,8,112]{2,1,0:T(8,128)S(1)} %slice.34), channel_id=1, source_target_pairs={{0,1},{1,2},{2,3},{3,4},{4,5},{5,6},{6,7},{7,8},{8,9},{9,10},{10,1... | collective-permute-start | bytes 86024 | tf_op jit(solution)/shard_map/ppermute | solution.py:25
  5.9 16.1 %collective-permute-start.16 = (f32[8,8,112]{2,1,0:T(8,128)S(1)}, f32[8,8,112]{2,1,0:T(8,128)S(1)}, u32[]{:S(2)}, u32[]{:S(2)}) collective-permute-start(f32[8,8,112]{2,1,0:T(8,128)S(1)} %slice.36), channel_id=1, source_target_pairs={{1,0},{2,1},{3,2},{4,3},{5,4},{6,5},{7,6},{8,7},{9,8},{10,9},{11,1... | collective-permute-start | bytes 86024 | tf_op jit(solution)/shard_map/ppermute | solution.py:26
  9.1 0.8 copy-start
  9.3 0.8 copy-start.3
  10.4 5.8 %collective-permute-start.1 = (f32[8,256]{1,0:T(8,128)S(1)}, f32[8,256]{1,0:T(8,128)S(1)}, u32[]{:S(2)}, u32[]{:S(2)}) collective-permute-start(f32[8,256]{1,0:T(8,128)S(1)} %collective-permute-done), channel_id=1, source_target_pairs={{0,1},{1,2},{2,3},{3,4},{4,5},{5,6},{6,7},{7,8},{8,9},{9,10},{10,1... | collective-permute-start | bytes 24584 | tf_op jit(solution)/shard_map/ppermute | solution.py:95
  16.2 5.8 %collective-permute-start.2 = (f32[8,256]{1,0:T(8,128)S(1)}, f32[8,256]{1,0:T(8,128)S(1)}, u32[]{:S(2)}, u32[]{:S(2)}) collective-permute-start(f32[8,256]{1,0:T(8,128)S(1)} %collective-permute-done.1), channel_id=1, source_target_pairs={{0,1},{1,2},{2,3},{3,4},{4,5},{5,6},{6,7},{7,8},{8,9},{9,10},{10,1... | collective-permute-start | bytes 24584 | tf_op jit(solution)/shard_map/ppermute | solution.py:95
  22.0 6.9 %collective-permute-start.3 = (f32[8,256]{1,0:T(8,128)S(1)}, f32[8,256]{1,0:T(8,128)S(1)}, u32[]{:S(2)}, u32[]{:S(2)}) collective-permute-start(f32[8,256]{1,0:T(8,128)S(1)} %collective-permute-done.2), channel_id=1, source_target_pairs={{0,1},{1,2},{2,3},{3,4},{4,5},{5,6},{6,7},{7,8},{8,9},{9,10},{10,1... | collective-permute-start | bytes 24584 | tf_op jit(solution)/shard_map/ppermute | solution.py:95
  28.9 5.8 %collective-permute-start.4 = (f32[8,256]{1,0:T(8,128)S(1)}, f32[8,256]{1,0:T(8,128)S(1)}, u32[]{:S(2)}, u32[]{:S(2)}) collective-permute-start(f32[8,256]{1,0:T(8,128)S(1)} %collective-permute-done.3), channel_id=1, source_target_pairs={{0,1},{1,2},{2,3},{3,4},{4,5},{5,6},{6,7},{7,8},{8,9},{9,10},{10,1... | collective-permute-start | bytes 24584 | tf_op jit(solution)/shard_map/ppermute | solution.py:95
  34.7 5.8 %collective-permute-start.5 = (f32[8,256]{1,0:T(8,128)S(1)}, f32[8,256]{1,0:T(8,128)S(1)}, u32[]{:S(2)}, u32[]{:S(2)}) collective-permute-start(f32[8,256]{1,0:T(8,128)S(1)} %collective-permute-done.4), channel_id=1, source_target_pairs={{0,1},{1,2},{2,3},{3,4},{4,5},{5,6},{6,7},{7,8},{8,9},{9,10},{10,1... | collective-permute-start | bytes 24584 | tf_op jit(solution)/shard_map/ppermute | solution.py:95
  40.5 5.8 %collective-permute-start.6 = (f32[8,256]{1,0:T(8,128)S(1)}, f32[8,256]{1,0:T(8,128)S(1)}, u32[]{:S(2)}, u32[]{:S(2)}) collective-permute-start(f32[8,256]{1,0:T(8,128)S(1)} %collective-permute-done.5), channel_id=1, source_target_pairs={{0,1},{1,2},{2,3},{3,4},{4,5},{5,6},{6,7},{7,8},{8,9},{9,10},{10,1... | collective-permute-start | bytes 24584 | tf_op jit(solution)/shard_map/ppermute | solution.py:95
  46.3 5.8 %collective-permute-start.7 = (f32[8,256]{1,0:T(8,128)S(1)}, f32[8,256]{1,0:T(8,128)S(1)}, u32[]{:S(2)}, u32[]{:S(2)}) collective-permute-start(f32[8,256]{1,0:T(8,128)S(1)} %collective-permute-done.6), channel_id=1, source_target_pairs={{0,1},{1,2},{2,3},{3,4},{4,5},{5,6},{6,7},{7,8},{8,9},{9,10},{10,1... | collective-permute-start | bytes 24584 | tf_op jit(solution)/shard_map/ppermute | solution.py:95
  52.0 5.8 %collective-permute-start.8 = (f32[8,256]{1,0:T(8,128)S(1)}, f32[8,256]{1,0:T(8,128)S(1)}, u32[]{:S(2)}, u32[]{:S(2)}) collective-permute-start(f32[8,256]{1,0:T(8,128)S(1)} %collective-permute-done.7), channel_id=1, source_target_pairs={{0,1},{1,2},{2,3},{3,4},{4,5},{5,6},{6,7},{7,8},{8,9},{9,10},{10,1... | collective-permute-start | bytes 24584 | tf_op jit(solution)/shard_map/ppermute | solution.py:95
  57.8 5.8 %collective-permute-start.9 = (f32[8,256]{1,0:T(8,128)S(1)}, f32[8,256]{1,0:T(8,128)S(1)}, u32[]{:S(2)}, u32[]{:S(2)}) collective-permute-start(f32[8,256]{1,0:T(8,128)S(1)} %collective-permute-done.8), channel_id=1, source_target_pairs={{0,1},{1,2},{2,3},{3,4},{4,5},{5,6},{6,7},{7,8},{8,9},{9,10},{10,1... | collective-permute-start | bytes 24584 | tf_op jit(solution)/shard_map/ppermute | solution.py:95
  63.6 5.8 %collective-permute-start.10 = (f32[8,256]{1,0:T(8,128)S(1)}, f32[8,256]{1,0:T(8,128)S(1)}, u32[]{:S(2)}, u32[]{:S(2)}) collective-permute-start(f32[8,256]{1,0:T(8,128)S(1)} %collective-permute-done.9), channel_id=1, source_target_pairs={{0,1},{1,2},{2,3},{3,4},{4,5},{5,6},{6,7},{7,8},{8,9},{9,10},{10,1... | collective-permute-start | bytes 24584 | tf_op jit(solution)/shard_map/ppermute | solution.py:95
  69.3 5.8 %collective-permute-start.11 = (f32[8,256]{1,0:T(8,128)S(1)}, f32[8,256]{1,0:T(8,128)S(1)}, u32[]{:S(2)}, u32[]{:S(2)}) collective-permute-start(f32[8,256]{1,0:T(8,128)S(1)} %collective-permute-done.10), channel_id=1, source_target_pairs={{0,1},{1,2},{2,3},{3,4},{4,5},{5,6},{6,7},{7,8},{8,9},{9,10},{10,1... | collective-permute-start | bytes 24584 | tf_op jit(solution)/shard_map/ppermute | solution.py:95
  75.1 5.8 %collective-permute-start.12 = (f32[8,256]{1,0:T(8,128)S(1)}, f32[8,256]{1,0:T(8,128)S(1)}, u32[]{:S(2)}, u32[]{:S(2)}) collective-permute-start(f32[8,256]{1,0:T(8,128)S(1)} %collective-permute-done.11), channel_id=1, source_target_pairs={{0,1},{1,2},{2,3},{3,4},{4,5},{5,6},{6,7},{7,8},{8,9},{9,10},{10,1... | collective-permute-start | bytes 24584 | tf_op jit(solution)/shard_map/ppermute | solution.py:95
  80.9 5.8 %collective-permute-start.13 = (f32[8,256]{1,0:T(8,128)S(1)}, f32[8,256]{1,0:T(8,128)S(1)}, u32[]{:S(2)}, u32[]{:S(2)}) collective-permute-start(f32[8,256]{1,0:T(8,128)S(1)} %collective-permute-done.12), channel_id=1, source_target_pairs={{0,1},{1,2},{2,3},{3,4},{4,5},{5,6},{6,7},{7,8},{8,9},{9,10},{10,1... | collective-permute-start | bytes 24584 | tf_op jit(solution)/shard_map/ppermute | solution.py:95
  86.7 5.8 %collective-permute-start.14 = (f32[8,256]{1,0:T(8,128)S(1)}, f32[8,256]{1,0:T(8,128)S(1)}, u32[]{:S(2)}, u32[]{:S(2)}) collective-permute-start(f32[8,256]{1,0:T(8,128)S(1)} %collective-permute-done.13), channel_id=1, source_target_pairs={{0,1},{1,2},{2,3},{3,4},{4,5},{5,6},{6,7},{7,8},{8,9},{9,10},{10,1... | collective-permute-start | bytes 24584 | tf_op jit(solution)/shard_map/ppermute | solution.py:95
